TPU v7x, 256 devices: a whole 4x4x8 slice. The times are simulated.
256 devices in a mesh: dp: 32 (over x, y, core), tensor: 8 (over z).
Axes of the slice: x: 4, y: 4, z: 8, core: 2. Of those that a mesh axis runs over, the one named last changes fastest.
Arguments:
- hidden_states: bfloat16 [24576, 4096], P('dp', 'tensor')
- neighbour_ids: int32 [384, 2], P('dp'), may hold values from 0 to 511, as said below
- database: bfloat16 [512, 128, 896], P('dp')
- w_up: bfloat16 [896, 3584], P(None, 'tensor'), may hold values from -0.1875 to 0.1875
- w_down: bfloat16 [3584, 896], P('tensor'), may hold values from -0.09375 to 0.09375
- w_query: bfloat16 [4096, 4096], P(None, 'tensor'), may hold values from -0.09375 to 0.09375
- w_key: bfloat16 [896, 4096], P(None, 'tensor'), may hold values from -0.1875 to 0.1875
- w_value: bfloat16 [896, 4096], P(None, 'tensor'), may hold values from -0.1875 to 0.1875
Outputs:
- attended: bfloat16 [24576, 4096], P('dp', 'tensor')
Inputs may be any that keep to these rules, and one draw needn't show every extreme that they name: `neighbour_ids`: block ids are grouped by owner: index s of dp holds blocks s * 16 to (s + 1) * 16 - 1. Among the 24 ids of one sequence, no owner's blocks are named more than 2 times; one owner, the same for every sequence, is named exactly 2 times by each.
All inputs are finite; a program needn't handle non-finite values.
Results may differ from a plain program's by a relative error of at most 0.02.
Values may be sent and summed in bfloat16 or wider, within the bound.
No kernel may reach another device: no remote copies, remote signals or barrier semaphores. Data moves between devices by JAX's collectives and lax.ppermute only.
A program may use at most 128 MiB of HBM per device.

v0:
```python
import math
import jax
import jax.numpy as jnp
from jax import lax
from jax.sharding import PartitionSpec as P

HD = 128
SPAN = 64
KN = 2
NTOK = 128
EPSILON = 1e-06
LOGIT_SCALE = 3.0


def head_norm(projected):
    shaped = projected.reshape(projected.shape[0], -1, HD)
    scaled = shaped * lax.rsqrt(jnp.mean(shaped * shaped, axis=-1, keepdims=True) + EPSILON)
    return scaled.astype(jnp.bfloat16)


def attend(queries, keys, values):
    heads_here = queries.shape[0]
    seq_rows = queries.shape[1] + SPAN - 1
    span_count = seq_rows // SPAN
    shifted = jnp.concatenate(
        [queries, jnp.zeros((heads_here, SPAN - 1, HD), jnp.bfloat16)], axis=1
    )
    windows = shifted.reshape(heads_here, span_count, SPAN, HD)
    key_blocks = keys.reshape(heads_here, span_count, KN * NTOK, HD)
    value_blocks = values.reshape(heads_here, span_count, KN * NTOK, HD)
    scores = jnp.einsum("hcqd,hckd->hcqk", windows, key_blocks, preferred_element_type=jnp.float32)
    scores = scores * (LOGIT_SCALE / math.sqrt(HD))
    expo = jnp.exp(scores)
    weights = (expo / jnp.sum(expo, axis=-1, keepdims=True)).astype(jnp.bfloat16)
    mixed = jnp.einsum("hcqk,hckd->cqhd", weights, value_blocks, preferred_element_type=jnp.float32)
    mixed = mixed.astype(jnp.bfloat16).reshape(seq_rows, heads_here * HD)
    leading = jnp.zeros((SPAN - 1, heads_here * HD), jnp.bfloat16)
    return jnp.concatenate([leading, mixed[: seq_rows - SPAN + 1]], axis=0)


def head_norm_major(projected):
    scaled = projected * lax.rsqrt(
        jnp.mean(projected * projected, axis=-1, keepdims=True) + EPSILON
    )
    return scaled.astype(jnp.bfloat16)


def ring_hops(states, n):
    to_right = [(i, (i + 1) % n) for i in range(n)]
    to_left = [(i, (i - 1) % n) for i in range(n)]
    going_right = states
    going_left = states
    right_hops = n // 2
    left_hops = n - 1 - right_hops
    steps = []
    for hop in range(1, right_hops + 1):
        step = {}
        going_right = lax.ppermute(going_right, "tensor", to_right)
        step[(n - hop) % n] = going_right
        if hop <= left_hops:
            going_left = lax.ppermute(going_left, "tensor", to_left)
            step[hop] = going_left
        steps.append(step)
    return steps


def ring_query(got, w_query, n):
    width = got[0].shape[1]
    me = lax.axis_index("tensor")
    total = None
    for offset in range(n):
        rows = lax.dynamic_slice_in_dim(w_query, (me + offset) % n * width, width, 0)
        term = jnp.dot(got[offset], rows, preferred_element_type=jnp.float32)
        total = term if total is None else total + term
    return total


def shards(hidden_states, neighbour_ids, database, w_up, w_down, w_query, w_key, w_value):
    dp_count = lax.axis_size("dp")
    tensor_count = lax.axis_size("tensor")
    shard_blocks = database.shape[0]
    block_tokens = database.shape[1]
    enc_width = database.shape[2]
    flat_ids = neighbour_ids.reshape(-1)
    request_count = flat_ids.shape[0]
    capacity = max(2, (request_count + dp_count - 1) // dp_count + 1)
    owners = flat_ids // shard_blocks
    local_rows = flat_ids % shard_blocks
    owner_match = (owners[:, None] == jnp.arange(dp_count, dtype=jnp.int32)[None, :]).astype(
        jnp.int32
    )
    positions = jnp.arange(request_count, dtype=jnp.int32)
    earlier = (positions[:, None] > positions[None, :]).astype(jnp.int32)
    ranks = jnp.sum(jnp.dot(earlier, owner_match) * owner_match, axis=1)
    slots = owners * capacity + ranks
    slot_match = slots[None, :] == jnp.arange(dp_count * capacity, dtype=jnp.int32)[:, None]
    requests = jnp.sum(jnp.where(slot_match, local_rows[None, :], 0), axis=1)
    requests = requests.reshape(dp_count, capacity)
    raw_float = database.astype(jnp.float32)
    normed = (
        raw_float * lax.rsqrt(jnp.mean(raw_float * raw_float, axis=-1, keepdims=True) + EPSILON)
    ).astype(jnp.bfloat16)
    inner = jnp.einsum("bte,ef->btf", normed, w_up, preferred_element_type=jnp.float32)
    active = jax.nn.gelu(inner).astype(jnp.bfloat16)
    partial = jnp.einsum("btf,fe->bte", active, w_down, preferred_element_type=jnp.float32)
    rows_here = block_tokens // tensor_count
    states = hidden_states[SPAN - 1 :]
    head_rows = 3 * SPAN
    head_got = {0: states[:head_rows]}
    for step in ring_hops(states[:head_rows], tensor_count):
        head_got.update(step)
    summed = lax.psum_scatter(
        partial.astype(jnp.bfloat16), "tensor", scatter_dimension=1, tiled=True
    )
    states_rest, summed, head_got = lax.optimization_barrier((states[head_rows:], summed, head_got))
    summed = summed.astype(jnp.float32)
    raw_own = lax.dynamic_slice_in_dim(
        raw_float, lax.axis_index("tensor") * rows_here, rows_here, 1
    )
    encoded_own = (raw_own + summed).astype(jnp.bfloat16)
    asked = lax.all_to_all(requests, "dp", split_axis=0, concat_axis=0, tiled=True)
    replies = lax.all_to_all(encoded_own[asked], "dp", split_axis=0, concat_axis=0, tiled=True)
    mine = replies.reshape(dp_count * capacity, rows_here, enc_width)[slots]
    encoded = lax.all_gather(mine, "tensor", axis=1, tiled=True)
    heads_here = w_query.shape[1] // HD
    states_rest = lax.all_gather(states_rest, "tensor", axis=1, tiled=True)
    projected = jnp.concatenate(
        [
            ring_query(head_got, w_query, tensor_count),
            jnp.dot(states_rest, w_query, preferred_element_type=jnp.float32),
        ],
        axis=0,
    )
    queries = head_norm_major(projected.reshape(projected.shape[0], heads_here, HD))
    queries = jnp.transpose(queries, (1, 0, 2))
    flat_encoded = encoded.reshape(-1, enc_width)
    keys = head_norm_major(
        jnp.einsum(
            "ke,ehd->hkd",
            flat_encoded,
            w_key.reshape(enc_width, heads_here, HD),
            preferred_element_type=jnp.float32,
        )
    )
    values = jnp.einsum(
        "ke,ehd->hkd",
        flat_encoded,
        w_value.reshape(enc_width, heads_here, HD),
        preferred_element_type=jnp.float32,
    ).astype(jnp.bfloat16)
    return attend(queries, keys, values)


def solution(mesh):
    in_specs = (
        P("dp", "tensor"),
        P("dp", None),
        P("dp", None, None),
        P(None, "tensor"),
        P("tensor", None),
        P(None, "tensor"),
        P(None, "tensor"),
        P(None, "tensor"),
    )
    out_specs = P("dp", "tensor")
    return jax.shard_map(shards, mesh=mesh, in_specs=in_specs, out_specs=out_specs, check_vma=False)
```

profile of v0, /device:TPU:1, one launch (start us, length us, event | category | flops | bytes accessed | tf_op | source)
XLA Modules:
  0.0 229.0 jit_solution(14006398751083424595)
XLA Ops:
  6.5 3.0 %multiply_reduce_fusion = f32[16,128]{1,0:T(8,128)S(1)} fusion(bf16[16,128,896]{2,1,0:T(8,128)(2,1)} %param.10), kind=kLoop, calls=%fused_computation.3 | loop fusion | flops 5502976 | bytes 3678208 | tf_op jit(solution)/shard_map/reduce_sum | solution.py:101
  9.6 7.7 %convolution_convert_fusion.1 = bf16[16,128,896]{2,1,0:T(8,128)(2,1)} fusion(f32[16,128]{1,0:T(8,128)S(1)} %add_rsqrt_fusion.2, bf16[16,128,896]{2,1,0:T(8,128)(2,1)} %param.10, bf16[448,896]{1,0:T(8,128)(2,1)S(1)} %copy-done.14, bf16[896,448]{0,1:T(8,128)(2,1)S(1)} %copy-done.15), kind=kOutput, calls=%fused_computation.26 | convolution fusion | flops 3303931904 | bytes 8953856 | tf_op jit(solution)/shard_map/btf,fe->bte/dot_general | solution.py:105
  18.4 2.5 %collective-permute-start.3 = (bf16[192,512]{1,0:T(8,128)(2,1)S(1)}, bf16[192,512]{1,0:T(8,128)(2,1)S(1)}, u32[]{:S(2)}, u32[]{:S(2)}) collective-permute-start(bf16[192,512]{1,0:T(8,128)(2,1)S(1)} %slice.14), channel_id=1, source_target_pairs={{0,1},{1,2},{2,3},{3,4},{4,5},{5,6},{6,7},{7,0},{8,9},{9,10},{10,1... | collective-permute-start | bytes 589832 | tf_op jit(solution)/shard_map/ppermute | solution.py:58
  21.0 4.0 %collective-permute-start = (bf16[192,512]{1,0:T(8,128)(2,1)S(1)}, bf16[192,512]{1,0:T(8,128)(2,1)S(1)}, u32[]{:S(2)}, u32[]{:S(2)}) collective-permute-start(bf16[192,512]{1,0:T(8,128)(2,1)S(1)} %slice.14), channel_id=1, source_target_pairs={{0,7},{1,0},{2,1},{3,2},{4,3},{5,4},{6,5},{7,6},{8,15},{9,8},{10,9... | collective-permute-start | bytes 589832 | tf_op jit(solution)/shard_map/ppermute | solution.py:61
  25.0 4.5 %collective-permute-done.3 = bf16[192,512]{1,0:T(8,128)(2,1)S(1)} collective-permute-done((bf16[192,512]{1,0:T(8,128)(2,1)S(1)}, bf16[192,512]{1,0:T(8,128)(2,1)S(1)}, u32[]{:S(2)}, u32[]{:S(2)}) %collective-permute-start.3) | collective-permute-done | bytes 196640 | tf_op jit(solution)/shard_map/ppermute | solution.py:58
  29.5 2.7 %collective-permute-start.1 = (bf16[192,512]{1,0:T(8,128)(2,1)S(1)}, bf16[192,512]{1,0:T(8,128)(2,1)S(1)}, u32[]{:S(2)}, u32[]{:S(2)}) collective-permute-start(bf16[192,512]{1,0:T(8,128)(2,1)S(1)} %collective-permute-done), channel_id=1, source_target_pairs={{0,7},{1,0},{2,1},{3,2},{4,3},{5,4},{6,5},{7,6},{8,15},{9,8},{10,9... | collective-permute-start | bytes 589832 | tf_op jit(solution)/shard_map/ppermute | solution.py:61
  32.2 3.7 %collective-permute-done.4 = bf16[192,512]{1,0:T(8,128)(2,1)S(1)} collective-permute-done((bf16[192,512]{1,0:T(8,128)(2,1)S(1)}, bf16[192,512]{1,0:T(8,128)(2,1)S(1)}, u32[]{:S(2)}, u32[]{:S(2)}) %collective-permute-start.4) | collective-permute-done | bytes 196640 | tf_op jit(solution)/shard_map/ppermute | solution.py:58
  35.9 4.0 %collective-permute-done.1 = bf16[192,512]{1,0:T(8,128)(2,1)S(1)} collective-permute-done((bf16[192,512]{1,0:T(8,128)(2,1)S(1)}, bf16[192,512]{1,0:T(8,128)(2,1)S(1)}, u32[]{:S(2)}, u32[]{:S(2)}) %collective-permute-start.1) | collective-permute-done | bytes 196640 | tf_op jit(solution)/shard_map/ppermute | solution.py:61
  39.9 3.5 %collective-permute-start.2 = (bf16[192,512]{1,0:T(8,128)(2,1)S(1)}, bf16[192,512]{1,0:T(8,128)(2,1)S(1)}, u32[]{:S(2)}, u32[]{:S(2)}) collective-permute-start(bf16[192,512]{1,0:T(8,128)(2,1)S(1)} %collective-permute-done.1), channel_id=1, source_target_pairs={{0,7},{1,0},{2,1},{3,2},{4,3},{5,4},{6,5},{7,6},{8,15},{9,8},{10,9... | collective-permute-start | bytes 589832 | tf_op jit(solution)/shard_map/ppermute | solution.py:61
  43.4 3.4 %collective-permute-done.5 = bf16[192,512]{1,0:T(8,128)(2,1)S(1)} collective-permute-done((bf16[192,512]{1,0:T(8,128)(2,1)S(1)}, bf16[192,512]{1,0:T(8,128)(2,1)S(1)}, u32[]{:S(2)}, u32[]{:S(2)}) %collective-permute-start.5) | collective-permute-done | bytes 196640 | tf_op jit(solution)/shard_map/ppermute | solution.py:58
  47.7 3.8 %collective-permute-done.2 = bf16[192,512]{1,0:T(8,128)(2,1)S(1)} collective-permute-done((bf16[192,512]{1,0:T(8,128)(2,1)S(1)}, bf16[192,512]{1,0:T(8,128)(2,1)S(1)}, u32[]{:S(2)}, u32[]{:S(2)}) %collective-permute-start.2) | collective-permute-done | bytes 196640 | tf_op jit(solution)/shard_map/ppermute | solution.py:61
  51.5 6.2 %collective-permute-done.6 = bf16[192,512]{1,0:T(8,128)(2,1)S(1)} collective-permute-done((bf16[192,512]{1,0:T(8,128)(2,1)S(1)}, bf16[192,512]{1,0:T(8,128)(2,1)S(1)}, u32[]{:S(2)}, u32[]{:S(2)}) %collective-permute-start.6) | collective-permute-done | bytes 196640 | tf_op jit(solution)/shard_map/ppermute | solution.py:58
  57.7 23.8 %reduce-scatter.2.cloned.1.call-done = bf16[16,16,896]{2,1,0:T(8,128)(2,1)} async-done(((bf16[16,128,896]{2,1,0:T(8,128)(2,1)}), bf16[16,16,896]{2,1,0:T(8,128)(2,1)}) %reduce-scatter.2.cloned.1.call-update) | async-done | bytes 458768 | tf_op jit(solution)/shard_map/reduce_scatter | solution.py:112
  82.8 7.6 %all-to-all-start = ((s32[32,1,2]{2,1,0:T(1,128)}), s32[32,1,2]{2,1,0:T(1,128)S(1)}, u32[]{:S(2)}, u32[]{:S(2)}) async-start(s32[32,1,2]{2,1,0:T(1,128)} %bitcast.2), calls=%async_computation.1 | async-start | bytes 32768 | tf_op jit(solution)/shard_map/all_to_all | solution.py:121
  90.5 5.8 %convert_element_type.41 = f32[16,128,896]{2,1,0:T(8,128)} convert(bf16[16,128,896]{2,1,0:T(8,128)(2,1)} %param.10) | non-fusion elementwise | flops 1835008 | bytes 11010048 | tf_op jit(solution)/shard_map/convert_element_type | solution.py:99
  97.7 1.3 add_convert_fusion
  98.9 2.0 gather_fusion
  100.9 6.4 %all-to-all-start.1 = ((bf16[32,2,16,896]{3,2,1,0:T(8,128)(2,1)}), bf16[32,2,16,896]{3,2,1,0:T(8,128)(2,1)S(1)}, u32[]{:S(2)}, u32[]{:S(2)}) async-start(bf16[32,2,16,896]{3,2,1,0:T(8,128)(2,1)} %bitcast.4), calls=%async_computation.2 | async-start | bytes 3670016 | tf_op jit(solution)/shard_map/all_to_all | solution.py:122
  107.7 25.2 %all-to-all-done.1 = bf16[32,2,16,896]{3,2,1,0:T(8,128)(2,1)S(1)} async-done(((bf16[32,2,16,896]{3,2,1,0:T(8,128)(2,1)}), bf16[32,2,16,896]{3,2,1,0:T(8,128)(2,1)S(1)}, u32[]{:S(2)}, u32[]{:S(2)}) %all-to-all-start.1) | async-done | bytes 1835040 | tf_op jit(solution)/shard_map/all_to_all | solution.py:122
  132.8 1.5 gather_fusion.1
  134.5 1.5 fusion.48
  136.0 1.4 fusion.50
  137.4 1.4 fusion.52
  138.8 1.3 fusion.54
  141.3 5.8 %fusion.77 = f32[513,512]{1,0:T(8,128)S(1)} fusion(bf16[513,4096]{1,0:T(8,128)(2,1)} %all-gather.4.cloned.1.call-done, bf16[4096,512]{1,0:T(8,128)(2,1)} %param.13), kind=kOutput, calls=%fused_computation.107 | convolution fusion | flops 2151677952 | bytes 9447424 | tf_op jit(solution)/shard_map/dot_general | solution.py:130
  148.5 1.7 reshape.246
  151.1 1.7 fusion.47
  152.9 52.7 %all-gather.6.cloned.1.call-done = bf16[24,128,896]{2,1,0:T(8,128)(2,1)} async-done(((bf16[24,16,896]{2,1,0:T(8,128)(2,1)}), bf16[24,128,896]{2,1,0:T(8,128)(2,1)}) %all-gather.6.cloned.1.call-update) | async-done | bytes 5505040 | tf_op jit(solution)/shard_map/all_gather | solution.py:124
  205.7 6.9 %fusion = (f32[4,3072]{1,0:T(4,128)S(1)}, f32[3072,4,128]{2,0,1:T(8,128)S(1)}) fusion(bf16[3072,896,1]{1,0,2:T(8,128)(2,1)} %bitcast.79, bf16[896,512]{1,0:T(8,128)(2,1)S(1)} %copy-done), kind=kOutput, calls=%fused_computation.6 | convolution fusion | flops 2821705728 | bytes 12763136 | tf_op jit(solution)/shard_map/ke,ehd->hkd/dot_general | solution.py:138
  212.6 3.6 %convolution_convert_fusion = bf16[3072,4,128]{2,0,1:T(8,128)(2,1)S(1)} fusion(bf16[3072,896,1]{1,0,2:T(8,128)(2,1)S(1)} %bitcast.80, bf16[896,512]{1,0:T(8,128)(2,1)S(1)} %copy-done.13), kind=kOutput, calls=%fused_computation.9 | convolution fusion | flops 2820145152 | bytes 9568256 | tf_op jit(solution)/shard_map/ke,ehd->hkd/dot_general | solution.py:145
  216.2 1.9 fusion.1
  218.2 1.3 fusion.15
  (77 shorter events, 11.6 us)
Async XLA Ops:
  6.5 199.1 %copy-start = (bf16[896,512]{1,0:T(8,128)(2,1)S(1)}, bf16[896,512]{1,0:T(8,128)(2,1)}, u32[]{:S(2)}) copy-start(bf16[896,512]{1,0:T(8,128)(2,1)} %param.14) | copy-start | bytes 2752516
  6.5 3.0 %copy-start.15 = (bf16[896,448]{0,1:T(8,128)(2,1)S(1)}, bf16[896,448]{0,1:T(8,128)(2,1)}, u32[]{:S(2)}) copy-start(bf16[896,448]{0,1:T(8,128)(2,1)} %param.11) | copy-start | bytes 2408452
  6.5 3.0 %copy-start.14 = (bf16[448,896]{1,0:T(8,128)(2,1)S(1)}, bf16[448,896]{1,0:T(8,128)(2,1)}, u32[]{:S(2)}) copy-start(bf16[448,896]{1,0:T(8,128)(2,1)} %param.12) | copy-start | bytes 2408452
  6.5 74.9 %reduce-scatter.2.cloned.1.call-start = ((), (), s32[]{:S(2)}) async-start(), calls=%async_computation.3 | async-start | bytes 4128768 | tf_op jit(solution)/shard_map/reduce_scatter | solution.py:112
  17.3 1.1 copy-start.3
  17.3 64.3 %copy-start.11 = (s32[12,2]{0,1:T(2,128)S(1)}, s32[12,2]{0,1:T(2,128)}, u32[]{:S(2)}) copy-start(s32[12,2]{0,1:T(2,128)} %param.9) | copy-start | bytes 292
  17.3 124.1 %all-gather.4.cloned.1.call-start = ((), (), s32[]{:S(2)}) async-start(), calls=%async_computation.4 | async-start | bytes 4792320 | tf_op jit(solution)/shard_map/all_gather | solution.py:126
  18.4 11.1 %collective-permute-start.3 = (bf16[192,512]{1,0:T(8,128)(2,1)S(1)}, bf16[192,512]{1,0:T(8,128)(2,1)S(1)}, u32[]{:S(2)}, u32[]{:S(2)}) collective-permute-start(bf16[192,512]{1,0:T(8,128)(2,1)S(1)} %slice.14), channel_id=1, source_target_pairs={{0,1},{1,2},{2,3},{3,4},{4,5},{5,6},{6,7},{7,0},{8,9},{9,10},{10,1... | collective-permute-start | bytes 589832 | tf_op jit(solution)/shard_map/ppermute | solution.py:58
  21.0 8.6 %collective-permute-start = (bf16[192,512]{1,0:T(8,128)(2,1)S(1)}, bf16[192,512]{1,0:T(8,128)(2,1)S(1)}, u32[]{:S(2)}, u32[]{:S(2)}) collective-permute-start(bf16[192,512]{1,0:T(8,128)(2,1)S(1)} %slice.14), channel_id=1, source_target_pairs={{0,7},{1,0},{2,1},{3,2},{4,3},{5,4},{6,5},{7,6},{8,15},{9,8},{10,9... | collective-permute-start | bytes 589832 | tf_op jit(solution)/shard_map/ppermute | solution.py:61
  29.5 6.4 %collective-permute-start.4 = (bf16[192,512]{1,0:T(8,128)(2,1)S(1)}, bf16[192,512]{1,0:T(8,128)(2,1)S(1)}, u32[]{:S(2)}, u32[]{:S(2)}) collective-permute-start(bf16[192,512]{1,0:T(8,128)(2,1)S(1)} %collective-permute-done.3), channel_id=1, source_target_pairs={{0,1},{1,2},{2,3},{3,4},{4,5},{5,6},{6,7},{7,0},{8,9},{9,10},{10,1... | collective-permute-start | bytes 589832 | tf_op jit(solution)/shard_map/ppermute | solution.py:58
  29.5 10.4 %collective-permute-start.1 = (bf16[192,512]{1,0:T(8,128)(2,1)S(1)}, bf16[192,512]{1,0:T(8,128)(2,1)S(1)}, u32[]{:S(2)}, u32[]{:S(2)}) collective-permute-start(bf16[192,512]{1,0:T(8,128)(2,1)S(1)} %collective-permute-done), channel_id=1, source_target_pairs={{0,7},{1,0},{2,1},{3,2},{4,3},{5,4},{6,5},{7,6},{8,15},{9,8},{10,9... | collective-permute-start | bytes 589832 | tf_op jit(solution)/shard_map/ppermute | solution.py:61
  35.9 54.5 %copy-start.5 = (bf16[192,512]{1,0:T(8,128)(2,1)}, bf16[192,512]{1,0:T(8,128)(2,1)S(1)}, u32[]{:S(2)}) copy-start(bf16[192,512]{1,0:T(8,128)(2,1)S(1)} %collective-permute-done.4) | copy-start | bytes 589828
  35.9 10.8 %collective-permute-start.5 = (bf16[192,512]{1,0:T(8,128)(2,1)S(1)}, bf16[192,512]{1,0:T(8,128)(2,1)S(1)}, u32[]{:S(2)}, u32[]{:S(2)}) collective-permute-start(bf16[192,512]{1,0:T(8,128)(2,1)S(1)} %collective-permute-done.4), channel_id=1, source_target_pairs={{0,1},{1,2},{2,3},{3,4},{4,5},{5,6},{6,7},{7,0},{8,9},{9,10},{10,1... | collective-permute-start | bytes 589832 | tf_op jit(solution)/shard_map/ppermute | solution.py:58
  39.9 11.6 %collective-permute-start.2 = (bf16[192,512]{1,0:T(8,128)(2,1)S(1)}, bf16[192,512]{1,0:T(8,128)(2,1)S(1)}, u32[]{:S(2)}, u32[]{:S(2)}) collective-permute-start(bf16[192,512]{1,0:T(8,128)(2,1)S(1)} %collective-permute-done.1), channel_id=1, source_target_pairs={{0,7},{1,0},{2,1},{3,2},{4,3},{5,4},{6,5},{7,6},{8,15},{9,8},{10,9... | collective-permute-start | bytes 589832 | tf_op jit(solution)/shard_map/ppermute | solution.py:61
  46.8 49.5 %copy-start.6 = (bf16[192,512]{1,0:T(8,128)(2,1)}, bf16[192,512]{1,0:T(8,128)(2,1)S(1)}, u32[]{:S(2)}) copy-start(bf16[192,512]{1,0:T(8,128)(2,1)S(1)} %collective-permute-done.5) | copy-start | bytes 589828
  46.8 10.9 %collective-permute-start.6 = (bf16[192,512]{1,0:T(8,128)(2,1)S(1)}, bf16[192,512]{1,0:T(8,128)(2,1)S(1)}, u32[]{:S(2)}, u32[]{:S(2)}) collective-permute-start(bf16[192,512]{1,0:T(8,128)(2,1)S(1)} %collective-permute-done.5), channel_id=1, source_target_pairs={{0,1},{1,2},{2,3},{3,4},{4,5},{5,6},{6,7},{7,0},{8,9},{9,10},{10,1... | collective-permute-start | bytes 589832 | tf_op jit(solution)/shard_map/ppermute | solution.py:58
  51.5 44.8 %copy-start.7 = (bf16[192,512]{1,0:T(8,128)(2,1)}, bf16[192,512]{1,0:T(8,128)(2,1)S(1)}, u32[]{:S(2)}) copy-start(bf16[192,512]{1,0:T(8,128)(2,1)S(1)} %collective-permute-done.2) | copy-start | bytes 589828
  57.7 38.7 %copy-start.9 = (bf16[192,512]{1,0:T(8,128)(2,1)}, bf16[192,512]{1,0:T(8,128)(2,1)S(1)}, u32[]{:S(2)}) copy-start(bf16[192,512]{1,0:T(8,128)(2,1)S(1)} %collective-permute-done.6) | copy-start | bytes 589828
  82.8 14.5 %all-to-all-start = ((s32[32,1,2]{2,1,0:T(1,128)}), s32[32,1,2]{2,1,0:T(1,128)S(1)}, u32[]{:S(2)}, u32[]{:S(2)}) async-start(s32[32,1,2]{2,1,0:T(1,128)} %bitcast.2), calls=%async_computation.1 | async-start | bytes 32768 | tf_op jit(solution)/shard_map/all_to_all | solution.py:121
  90.5 7.2 %copy-start.4 = (bf16[16,16,896]{2,1,0:T(8,128)(2,1)S(1)}, bf16[16,16,896]{2,1,0:T(8,128)(2,1)}, u32[]{:S(2)}) copy-start(bf16[16,16,896]{2,1,0:T(8,128)(2,1)} %reduce-scatter.2.cloned.1.call-done) | copy-start | bytes 1376260
  100.9 31.9 %all-to-all-start.1 = ((bf16[32,2,16,896]{3,2,1,0:T(8,128)(2,1)}), bf16[32,2,16,896]{3,2,1,0:T(8,128)(2,1)S(1)}, u32[]{:S(2)}, u32[]{:S(2)}) async-start(bf16[32,2,16,896]{3,2,1,0:T(8,128)(2,1)} %bitcast.4), calls=%async_computation.2 | async-start | bytes 3670016 | tf_op jit(solution)/shard_map/all_to_all | solution.py:122
  107.3 98.3 %all-gather.6.cloned.1.call-start = ((), (), s32[]{:S(2)}) async-start(), calls=%async_computation.5 | async-start | bytes 6193152 | tf_op jit(solution)/shard_map/all_gather | solution.py:124
  134.3 4.5 %copy-start.10 = (bf16[192,512]{1,0:T(8,128)(2,1)S(1)}, bf16[192,512]{1,0:T(8,128)(2,1)}, u32[]{:S(2)}) copy-start(bf16[192,512]{1,0:T(8,128)(2,1)} %copy-done.9) | copy-start | bytes 589828
  134.3 5.8 %copy-start.8 = (bf16[192,512]{1,0:T(8,128)(2,1)S(1)}, bf16[192,512]{1,0:T(8,128)(2,1)}, u32[]{:S(2)}) copy-start(bf16[192,512]{1,0:T(8,128)(2,1)} %copy-done.7) | copy-start | bytes 589828
  134.5 5.7 %copy-start.2 = (bf16[4096,512]{1,0:T(8,128)(2,1)S(1)}, bf16[4096,512]{1,0:T(8,128)(2,1)}, u32[]{:S(2)}) copy-start(bf16[4096,512]{1,0:T(8,128)(2,1)} %param.13) | copy-start | bytes 12582916
  205.7 6.9 %copy-start.12 = (bf16[24,128,896]{2,1,0:T(8,128)(2,1)S(1)}, bf16[24,128,896]{2,1,0:T(8,128)(2,1)}, u32[]{:S(2)}) copy-start(bf16[24,128,896]{2,1,0:T(8,128)(2,1)} %all-gather.6.cloned.1.call-done) | copy-start | bytes 16515076
  205.7 6.9 %copy-start.13 = (bf16[896,512]{1,0:T(8,128)(2,1)S(1)}, bf16[896,512]{1,0:T(8,128)(2,1)}, u32[]{:S(2)}) copy-start(bf16[896,512]{1,0:T(8,128)(2,1)} %param.15) | copy-start | bytes 2752516
  219.5 3.0 %copy-start.1 = (bf16[896,512]{1,0:T(8,128)(2,1)S(1)}, bf16[896,512]{1,0:T(8,128)(2,1)}, u32[]{:S(2)}) copy-start(bf16[896,512]{1,0:T(8,128)(2,1)} %param.14) | copy-start | bytes 2752516
Sparse Core Ops, SparseCore 0:
  17.4 64.0 reduce-scatter.1
  83.3 54.8 all-gather.3
  139.9 65.6 all-gather.5
where the time goes:
time: 229 us
  waiting for transfers between devices  128 us (56%)
  matrix products  33.5 us (15%)
  starting transfers between devices  27 us (12%)
  other arithmetic  16 us (7%)
  between operations  13.6 us (6%)
  local copies, waits for them, and re-layouts  10.6 us (5%)
    all_gather x1, waiting for transfers between devices, shards(): encoded = lax.all_gather(mine, 'tensor', axis=1, tiled=True)  52.7 us
    all_to_all x1, waiting for transfers between devices, shards(): lax.all_to_all(encoded_own[asked], 'dp', split_axis=0, concat_axis=0, til...  25.2 us
    reduce_scatter x1, waiting for transfers between devices, shards(): lax.psum_scatter(partial.astype(jnp.bfloat16), 'tensor', scatter_dimensio...  23.8 us
    ppermute x4, waiting for transfers between devices, ring_hops(): going_right = lax.ppermute(going_right, 'tensor', to_right)  17.8 us
    ppermute x3, starting transfers between devices, ring_hops(): going_left = lax.ppermute(going_left, 'tensor', to_left)  10.2 us
    ppermute x3, waiting for transfers between devices, ring_hops(): going_left = lax.ppermute(going_left, 'tensor', to_left)  7.73 us
    dot_general x1, matrix products, shards(): jnp.einsum('btf,fe->bte', active, w_down, preferred_element_type=jnp.floa...  7.69 us
    all_to_all x1, starting transfers between devices, shards(): lax.all_to_all(requests, 'dp', split_axis=0, concat_axis=0, tiled=True)  7.59 us
  transfers between devices with their start and end apart: 12, of which 10 were waited for; matrix products, arithmetic and copies ran while one was open for 13% of the time, Pallas kernels for 0%

commit v1 on v0

--- a/solution.py
+++ b/solution.py
@@ -121,7 +121,24 @@
     asked = lax.all_to_all(requests, "dp", split_axis=0, concat_axis=0, tiled=True)
     replies = lax.all_to_all(encoded_own[asked], "dp", split_axis=0, concat_axis=0, tiled=True)
     mine = replies.reshape(dp_count * capacity, rows_here, enc_width)[slots]
-    encoded = lax.all_gather(mine, "tensor", axis=1, tiled=True)
+    size, index, rows_2 = (lax.axis_size("tensor"), lax.axis_index("tensor"), mine.shape[1])
+    forward = [(i_2, (i_2 + 1) % size) for i_2 in range(size)]
+    backward = [(i_2, (i_2 - 1) % size) for i_2 in range(size)]
+    result = jnp.zeros((*mine.shape[:1], size * rows_2, *mine.shape[1 + 1 :]), mine.dtype)
+    result = lax.dynamic_update_slice_in_dim(result, mine, index * rows_2, axis=1)
+    from_left = from_right = mine
+    middle = size // 2
+    for hop_2 in range(1, middle + 1):
+        from_left = lax.ppermute(from_left, "tensor", forward)
+        result = lax.dynamic_update_slice_in_dim(
+            result, from_left, (index - hop_2) % size * rows_2, axis=1
+        )
+        if hop_2 < size - middle:
+            from_right = lax.ppermute(from_right, "tensor", backward)
+            result = lax.dynamic_update_slice_in_dim(
+                result, from_right, (index + hop_2) % size * rows_2, axis=1
+            )
+    encoded = result
     heads_here = w_query.shape[1] // HD
     states_rest = lax.all_gather(states_rest, "tensor", axis=1, tiled=True)
     projected = jnp.concatenate(

time: 229 us -> 251 us (1.096); the launches traced: 229 us -> 248 us
  starting transfers between devices: 27 us -> 40.6 us
  waiting for transfers between devices: 128 us -> 131 us
    ppermute x0 -> x7, waiting for transfers between devices: none -> 76.2 us  [the longest x4 76.2 us: shards(): from_left = lax.ppermute(from_left, 'tensor', forward)]
    all_gather x1 -> x0, waiting for transfers between devices: 52.7 us -> none  [shards(): encoded = lax.all_gather(mine, 'tensor', axis=1, tiled=True)]
    reduce_scatter x1, waiting for transfers between devices: 23.8 us -> 9.44 us  [shards(): lax.psum_scatter(partial.astype(jnp.bfloat16), 'tensor', scatter_dimensio...]
    ppermute x0 -> x7, starting transfers between devices: none -> 8.26 us  [the longest x3 7.99 us: shards(): from_right = lax.ppermute(from_right, 'tensor', backward)]
    ppermute x4, waiting for transfers between devices: 17.8 us -> 11.4 us  [ring_hops(): going_right = lax.ppermute(going_right, 'tensor', to_right)]
    all_to_all x1, starting transfers between devices: 7.59 us -> 12.4 us  [shards(): lax.all_to_all(requests, 'dp', split_axis=0, concat_axis=0, tiled=True)]
  transfers between devices with their start and end apart: 12 -> 18, of which waited for: 10 -> 11; matrix products, arithmetic and copies ran while one was open for 13% -> 12% of each run, Pallas kernels for 0% -> 0%
where the time goes in v1:
time: 251 us; the launch traced here: 248 us
  waiting for transfers between devices  131 us (52%)
  starting transfers between devices  40.6 us (16%)
  matrix products  32.5 us (13%)
  other arithmetic  17.4 us (7%)
  between operations  14.2 us (6%)
  local copies, waits for them, and re-layouts  12.8 us (5%)
    ppermute x4, waiting for transfers between devices, shards(): from_left = lax.ppermute(from_left, 'tensor', forward)  76.2 us
    all_to_all x1, waiting for transfers between devices, shards(): lax.all_to_all(encoded_own[asked], 'dp', split_axis=0, concat_axis=0, til...  24.7 us
    all_to_all x1, starting transfers between devices, shards(): lax.all_to_all(requests, 'dp', split_axis=0, concat_axis=0, tiled=True)  12.4 us
    ppermute x4, waiting for transfers between devices, ring_hops(): going_right = lax.ppermute(going_right, 'tensor', to_right)  11.4 us
    ppermute x3, starting transfers between devices, ring_hops(): going_left = lax.ppermute(going_left, 'tensor', to_left)  9.77 us
    reduce_scatter x1, waiting for transfers between devices, shards(): lax.psum_scatter(partial.astype(jnp.bfloat16), 'tensor', scatter_dimensio...  9.44 us
    ppermute x3, waiting for transfers between devices, ring_hops(): going_left = lax.ppermute(going_left, 'tensor', to_left)  8.2 us
    ppermute x3, starting transfers between devices, shards(): from_right = lax.ppermute(from_right, 'tensor', backward)  7.99 us
  transfers between devices with their start and end apart: 18, of which 11 were waited for; matrix products, arithmetic and copies ran while one was open for 12% of the time, Pallas kernels for 0%

profile of v1, /device:TPU:1, one launch (start us, length us, event | category | flops | bytes accessed | tf_op | source)
XLA Modules:
  0.0 248.4 jit_solution(14088362952791232873)
XLA Ops:
  6.5 3.0 %multiply_reduce_fusion = f32[16,128]{1,0:T(8,128)S(1)} fusion(bf16[16,128,896]{2,1,0:T(8,128)(2,1)} %param.10), kind=kLoop, calls=%fused_computation.3 | loop fusion | flops 5502976 | bytes 3678208 | tf_op jit(solution)/shard_map/reduce_sum | solution.py:101
  9.6 7.7 %convolution_convert_fusion.1 = bf16[16,128,896]{2,1,0:T(8,128)(2,1)} fusion(f32[16,128]{1,0:T(8,128)S(1)} %add_rsqrt_fusion.2, bf16[16,128,896]{2,1,0:T(8,128)(2,1)} %param.10, bf16[448,896]{1,0:T(8,128)(2,1)S(1)} %copy-done.19, bf16[896,448]{0,1:T(8,128)(2,1)S(1)} %copy-done.20), kind=kOutput, calls=%fused_computation.26 | convolution fusion | flops 3303931904 | bytes 8953856 | tf_op jit(solution)/shard_map/btf,fe->bte/dot_general | solution.py:105
  18.4 2.5 %collective-permute-start.3 = (bf16[192,512]{1,0:T(8,128)(2,1)S(1)}, bf16[192,512]{1,0:T(8,128)(2,1)S(1)}, u32[]{:S(2)}, u32[]{:S(2)}) collective-permute-start(bf16[192,512]{1,0:T(8,128)(2,1)S(1)} %slice.14), channel_id=1, source_target_pairs={{0,1},{1,2},{2,3},{3,4},{4,5},{5,6},{6,7},{7,0},{8,9},{9,10},{10,1... | collective-permute-start | bytes 589832 | tf_op jit(solution)/shard_map/ppermute | solution.py:58
  21.0 4.0 %collective-permute-start = (bf16[192,512]{1,0:T(8,128)(2,1)S(1)}, bf16[192,512]{1,0:T(8,128)(2,1)S(1)}, u32[]{:S(2)}, u32[]{:S(2)}) collective-permute-start(bf16[192,512]{1,0:T(8,128)(2,1)S(1)} %slice.14), channel_id=1, source_target_pairs={{0,7},{1,0},{2,1},{3,2},{4,3},{5,4},{6,5},{7,6},{8,15},{9,8},{10,9... | collective-permute-start | bytes 589832 | tf_op jit(solution)/shard_map/ppermute | solution.py:61
  25.2 4.3 %collective-permute-done.3 = bf16[192,512]{1,0:T(8,128)(2,1)S(1)} collective-permute-done((bf16[192,512]{1,0:T(8,128)(2,1)S(1)}, bf16[192,512]{1,0:T(8,128)(2,1)S(1)}, u32[]{:S(2)}, u32[]{:S(2)}) %collective-permute-start.3) | collective-permute-done | bytes 196640 | tf_op jit(solution)/shard_map/ppermute | solution.py:58
  29.9 2.7 %collective-permute-start.1 = (bf16[192,512]{1,0:T(8,128)(2,1)S(1)}, bf16[192,512]{1,0:T(8,128)(2,1)S(1)}, u32[]{:S(2)}, u32[]{:S(2)}) collective-permute-start(bf16[192,512]{1,0:T(8,128)(2,1)S(1)} %collective-permute-done), channel_id=1, source_target_pairs={{0,7},{1,0},{2,1},{3,2},{4,3},{5,4},{6,5},{7,6},{8,15},{9,8},{10,9... | collective-permute-start | bytes 589832 | tf_op jit(solution)/shard_map/ppermute | solution.py:61
  32.6 3.3 %collective-permute-done.4 = bf16[192,512]{1,0:T(8,128)(2,1)S(1)} collective-permute-done((bf16[192,512]{1,0:T(8,128)(2,1)S(1)}, bf16[192,512]{1,0:T(8,128)(2,1)S(1)}, u32[]{:S(2)}, u32[]{:S(2)}) %collective-permute-start.4) | collective-permute-done | bytes 196640 | tf_op jit(solution)/shard_map/ppermute | solution.py:58
  36.8 12.4 %all-to-all-start = ((s32[32,1,2]{2,1,0:T(1,128)}), s32[32,1,2]{2,1,0:T(1,128)S(1)}, u32[]{:S(2)}, u32[]{:S(2)}) async-start(s32[32,1,2]{2,1,0:T(1,128)} %bitcast.2), calls=%async_computation.1 | async-start | bytes 32768 | tf_op jit(solution)/shard_map/all_to_all | solution.py:121
  50.1 5.8 %convert_element_type.41 = f32[16,128,896]{2,1,0:T(8,128)} convert(bf16[16,128,896]{2,1,0:T(8,128)(2,1)} %param.10) | non-fusion elementwise | flops 1835008 | bytes 11010048 | tf_op jit(solution)/shard_map/convert_element_type | solution.py:99
  56.2 3.0 %collective-permute-start.2 = (bf16[192,512]{1,0:T(8,128)(2,1)S(1)}, bf16[192,512]{1,0:T(8,128)(2,1)S(1)}, u32[]{:S(2)}, u32[]{:S(2)}) collective-permute-start(bf16[192,512]{1,0:T(8,128)(2,1)S(1)} %collective-permute-done.1), channel_id=1, source_target_pairs={{0,7},{1,0},{2,1},{3,2},{4,3},{5,4},{6,5},{7,6},{8,15},{9,8},{10,9... | collective-permute-start | bytes 589832 | tf_op jit(solution)/shard_map/ppermute | solution.py:61
  59.4 8.2 %collective-permute-done.2 = bf16[192,512]{1,0:T(8,128)(2,1)S(1)} collective-permute-done((bf16[192,512]{1,0:T(8,128)(2,1)S(1)}, bf16[192,512]{1,0:T(8,128)(2,1)S(1)}, u32[]{:S(2)}, u32[]{:S(2)}) %collective-permute-start.2) | collective-permute-done | bytes 196640 | tf_op jit(solution)/shard_map/ppermute | solution.py:61
  67.6 3.7 %collective-permute-done.6 = bf16[192,512]{1,0:T(8,128)(2,1)S(1)} collective-permute-done((bf16[192,512]{1,0:T(8,128)(2,1)S(1)}, bf16[192,512]{1,0:T(8,128)(2,1)S(1)}, u32[]{:S(2)}, u32[]{:S(2)}) %collective-permute-start.6) | collective-permute-done | bytes 196640 | tf_op jit(solution)/shard_map/ppermute | solution.py:58
  72.0 9.4 %reduce-scatter.2.cloned.1.call-done = bf16[16,16,896]{2,1,0:T(8,128)(2,1)} async-done(((bf16[16,128,896]{2,1,0:T(8,128)(2,1)}), bf16[16,16,896]{2,1,0:T(8,128)(2,1)}) %reduce-scatter.2.cloned.1.call-update) | async-done | bytes 458768 | tf_op jit(solution)/shard_map/reduce_scatter | solution.py:112
  82.9 2.0 gather_fusion
  84.9 7.6 %all-to-all-start.1 = ((bf16[32,2,16,896]{3,2,1,0:T(8,128)(2,1)}), bf16[32,2,16,896]{3,2,1,0:T(8,128)(2,1)S(1)}, u32[]{:S(2)}, u32[]{:S(2)}) async-start(bf16[32,2,16,896]{3,2,1,0:T(8,128)(2,1)} %bitcast.4), calls=%async_computation.2 | async-start | bytes 3670016 | tf_op jit(solution)/shard_map/all_to_all | solution.py:122
  93.4 24.7 %all-to-all-done.1 = bf16[32,2,16,896]{3,2,1,0:T(8,128)(2,1)S(1)} async-done(((bf16[32,2,16,896]{3,2,1,0:T(8,128)(2,1)}), bf16[32,2,16,896]{3,2,1,0:T(8,128)(2,1)S(1)}, u32[]{:S(2)}, u32[]{:S(2)}) %all-to-all-start.1) | async-done | bytes 1835040 | tf_op jit(solution)/shard_map/all_to_all | solution.py:122
  119.3 1.6 fusion.60
  120.8 1.4 fusion.58
  122.3 2.5 %collective-permute-start.8 = (bf16[24,16,896]{2,1,0:T(8,128)(2,1)S(1)}, bf16[24,16,896]{2,1,0:T(8,128)(2,1)S(1)}, u32[]{:S(2)}, u32[]{:S(2)}) collective-permute-start(bf16[24,16,896]{2,1,0:T(8,128)(2,1)S(1)} %gather_fusion.1), channel_id=1, source_target_pairs={{0,7},{1,0},{2,1},{3,2},{4,3},{5,4},{6,5},{7,6},{8,15},{9,8},{10,9... | collective-permute-start | bytes 2064392 | tf_op jit(solution)/shard_map/ppermute | solution.py:137
  124.8 27.5 %collective-permute-done.7 = bf16[24,16,896]{2,1,0:T(8,128)(2,1)S(1)} collective-permute-done((bf16[24,16,896]{2,1,0:T(8,128)(2,1)S(1)}, bf16[24,16,896]{2,1,0:T(8,128)(2,1)S(1)}, u32[]{:S(2)}, u32[]{:S(2)}) %collective-permute-start.7) | collective-permute-done | bytes 688160 | tf_op jit(solution)/shard_map/ppermute | solution.py:132
  153.7 1.4 fusion.54
  155.5 2.8 %collective-permute-start.10 = (bf16[24,16,896]{2,1,0:T(8,128)(2,1)S(1)}, bf16[24,16,896]{2,1,0:T(8,128)(2,1)S(1)}, u32[]{:S(2)}, u32[]{:S(2)}) collective-permute-start(bf16[24,16,896]{2,1,0:T(8,128)(2,1)S(1)} %collective-permute-done.8), channel_id=1, source_target_pairs={{0,7},{1,0},{2,1},{3,2},{4,3},{5,4},{6,5},{7,6},{8,15},{9,8},{10,9... | collective-permute-start | bytes 2064392 | tf_op jit(solution)/shard_map/ppermute | solution.py:137
  158.2 20.4 %collective-permute-done.9 = bf16[24,16,896]{2,1,0:T(8,128)(2,1)S(1)} collective-permute-done((bf16[24,16,896]{2,1,0:T(8,128)(2,1)S(1)}, bf16[24,16,896]{2,1,0:T(8,128)(2,1)S(1)}, u32[]{:S(2)}, u32[]{:S(2)}) %collective-permute-start.9) | collective-permute-done | bytes 688160 | tf_op jit(solution)/shard_map/ppermute | solution.py:132
  179.5 2.7 %collective-permute-start.12 = (bf16[24,16,896]{2,1,0:T(8,128)(2,1)S(1)}, bf16[24,16,896]{2,1,0:T(8,128)(2,1)S(1)}, u32[]{:S(2)}, u32[]{:S(2)}) collective-permute-start(bf16[24,16,896]{2,1,0:T(8,128)(2,1)S(1)} %collective-permute-done.10), channel_id=1, source_target_pairs={{0,7},{1,0},{2,1},{3,2},{4,3},{5,4},{6,5},{7,6},{8,15},{9,8},{10,9... | collective-permute-start | bytes 2064392 | tf_op jit(solution)/shard_map/ppermute | solution.py:137
  183.2 12.7 %collective-permute-done.11 = bf16[24,16,896]{2,1,0:T(8,128)(2,1)S(1)} collective-permute-done((bf16[24,16,896]{2,1,0:T(8,128)(2,1)S(1)}, bf16[24,16,896]{2,1,0:T(8,128)(2,1)S(1)}, u32[]{:S(2)}, u32[]{:S(2)}) %collective-permute-start.11) | collective-permute-done | bytes 688160 | tf_op jit(solution)/shard_map/ppermute | solution.py:132
  196.6 15.6 %collective-permute-done.13 = bf16[24,16,896]{2,1,0:T(8,128)(2,1)S(1)} collective-permute-done((bf16[24,16,896]{2,1,0:T(8,128)(2,1)S(1)}, bf16[24,16,896]{2,1,0:T(8,128)(2,1)S(1)}, u32[]{:S(2)}, u32[]{:S(2)}) %collective-permute-start.13) | collective-permute-done | bytes 688160 | tf_op jit(solution)/shard_map/ppermute | solution.py:132
  212.4 4.4 %fusion = (f32[4,3072]{1,0:T(4,128)S(1)}, f32[3072,4,128]{2,0,1:T(8,128)S(1)}) fusion(bf16[3072,896,1]{1,0,2:T(8,128)(2,1)S(1)} %bitcast.75, bf16[896,512]{1,0:T(8,128)(2,1)S(1)} %copy-done), kind=kOutput, calls=%fused_computation.6 | convolution fusion | flops 2821705728 | bytes 12763136 | tf_op jit(solution)/shard_map/ke,ehd->hkd/dot_general | solution.py:155
  216.8 5.0 %convolution_convert_fusion = bf16[3072,4,128]{2,0,1:T(8,128)(2,1)} fusion(bf16[3072,896,1]{1,0,2:T(8,128)(2,1)S(1)} %bitcast.76, bf16[896,512]{1,0:T(8,128)(2,1)S(1)} %copy-done.18), kind=kOutput, calls=%fused_computation.9 | convolution fusion | flops 2820145152 | bytes 9568256 | tf_op jit(solution)/shard_map/ke,ehd->hkd/dot_general | solution.py:162
  221.8 3.3 %fusion.1 = bf16[4,3072,128]{2,1,0:T(8,128)(2,1)} fusion(f32[3072,4,128]{2,0,1:T(8,128)S(1)} %get-tuple-element.28, f32[4,3072]{1,0:T(4,128)S(1)} %add_rsqrt_fusion.1), kind=kLoop, calls=%fused_computation.7 | loop fusion | flops 3145728 | bytes 9486336 | tf_op jit(solution)/shard_map/convert_element_type | solution.py:45
  225.1 5.8 %fusion.77 = f32[513,512]{1,0:T(8,128)S(1)} fusion(bf16[513,4096]{1,0:T(8,128)(2,1)} %all-gather.2.cloned.1.call-done, bf16[4096,512]{1,0:T(8,128)(2,1)} %param.13), kind=kOutput, calls=%fused_computation.115 | convolution fusion | flops 2151677952 | bytes 9447424 | tf_op jit(solution)/shard_map/dot_general | solution.py:147
  232.2 1.7 reshape.246
  234.8 1.7 fusion.47
  (109 shorter events, 19.2 us)
Async XLA Ops:
  6.5 205.8 %copy-start = (bf16[896,512]{1,0:T(8,128)(2,1)S(1)}, bf16[896,512]{1,0:T(8,128)(2,1)}, u32[]{:S(2)}) copy-start(bf16[896,512]{1,0:T(8,128)(2,1)} %param.14) | copy-start | bytes 2752516
  6.5 74.9 %reduce-scatter.2.cloned.1.call-start = ((), (), s32[]{:S(2)}) async-start(), calls=%async_computation.3 | async-start | bytes 4128768 | tf_op jit(solution)/shard_map/reduce_scatter | solution.py:112
  17.3 7.8 %copy-start.17 = (s32[12,2]{0,1:T(2,128)S(1)}, s32[12,2]{0,1:T(2,128)}, u32[]{:S(2)}) copy-start(s32[12,2]{0,1:T(2,128)} %param.9) | copy-start | bytes 292
  18.4 37.5 %copy-start.4 = (bf16[192,512]{1,0:T(8,128)(2,1)}, bf16[192,512]{1,0:T(8,128)(2,1)S(1)}, u32[]{:S(2)}) copy-start(bf16[192,512]{1,0:T(8,128)(2,1)S(1)} %slice.14) | copy-start | bytes 589828
  18.4 11.1 %collective-permute-start.3 = (bf16[192,512]{1,0:T(8,128)(2,1)S(1)}, bf16[192,512]{1,0:T(8,128)(2,1)S(1)}, u32[]{:S(2)}, u32[]{:S(2)}) collective-permute-start(bf16[192,512]{1,0:T(8,128)(2,1)S(1)} %slice.14), channel_id=1, source_target_pairs={{0,1},{1,2},{2,3},{3,4},{4,5},{5,6},{6,7},{7,0},{8,9},{9,10},{10,1... | collective-permute-start | bytes 589832 | tf_op jit(solution)/shard_map/ppermute | solution.py:58
  21.0 8.9 %collective-permute-start = (bf16[192,512]{1,0:T(8,128)(2,1)S(1)}, bf16[192,512]{1,0:T(8,128)(2,1)S(1)}, u32[]{:S(2)}, u32[]{:S(2)}) collective-permute-start(bf16[192,512]{1,0:T(8,128)(2,1)S(1)} %slice.14), channel_id=1, source_target_pairs={{0,7},{1,0},{2,1},{3,2},{4,3},{5,4},{6,5},{7,6},{8,15},{9,8},{10,9... | collective-permute-start | bytes 589832 | tf_op jit(solution)/shard_map/ppermute | solution.py:61
  29.5 26.4 %copy-start.7 = (bf16[192,512]{1,0:T(8,128)(2,1)}, bf16[192,512]{1,0:T(8,128)(2,1)S(1)}, u32[]{:S(2)}) copy-start(bf16[192,512]{1,0:T(8,128)(2,1)S(1)} %collective-permute-done.3) | copy-start | bytes 589828
  29.5 6.4 %collective-permute-start.4 = (bf16[192,512]{1,0:T(8,128)(2,1)S(1)}, bf16[192,512]{1,0:T(8,128)(2,1)S(1)}, u32[]{:S(2)}, u32[]{:S(2)}) collective-permute-start(bf16[192,512]{1,0:T(8,128)(2,1)S(1)} %collective-permute-done.3), channel_id=1, source_target_pairs={{0,1},{1,2},{2,3},{3,4},{4,5},{5,6},{6,7},{7,0},{8,9},{9,10},{10,1... | collective-permute-start | bytes 589832 | tf_op jit(solution)/shard_map/ppermute | solution.py:58
  29.8 26.1 %copy-start.11 = (bf16[192,512]{1,0:T(8,128)(2,1)}, bf16[192,512]{1,0:T(8,128)(2,1)S(1)}, u32[]{:S(2)}) copy-start(bf16[192,512]{1,0:T(8,128)(2,1)S(1)} %collective-permute-done) | copy-start | bytes 589828
  29.9 26.4 %collective-permute-start.1 = (bf16[192,512]{1,0:T(8,128)(2,1)S(1)}, bf16[192,512]{1,0:T(8,128)(2,1)S(1)}, u32[]{:S(2)}, u32[]{:S(2)}) collective-permute-start(bf16[192,512]{1,0:T(8,128)(2,1)S(1)} %collective-permute-done), channel_id=1, source_target_pairs={{0,7},{1,0},{2,1},{3,2},{4,3},{5,4},{6,5},{7,6},{8,15},{9,8},{10,9... | collective-permute-start | bytes 589832 | tf_op jit(solution)/shard_map/ppermute | solution.py:61
  35.9 20.0 %copy-start.9 = (bf16[192,512]{1,0:T(8,128)(2,1)}, bf16[192,512]{1,0:T(8,128)(2,1)S(1)}, u32[]{:S(2)}) copy-start(bf16[192,512]{1,0:T(8,128)(2,1)S(1)} %collective-permute-done.4) | copy-start | bytes 589828
  35.9 23.3 %collective-permute-start.5 = (bf16[192,512]{1,0:T(8,128)(2,1)S(1)}, bf16[192,512]{1,0:T(8,128)(2,1)S(1)}, u32[]{:S(2)}, u32[]{:S(2)}) collective-permute-start(bf16[192,512]{1,0:T(8,128)(2,1)S(1)} %collective-permute-done.4), channel_id=1, source_target_pairs={{0,1},{1,2},{2,3},{3,4},{4,5},{5,6},{6,7},{7,0},{8,9},{9,10},{10,1... | collective-permute-start | bytes 589832 | tf_op jit(solution)/shard_map/ppermute | solution.py:58
  36.8 19.4 %all-to-all-start = ((s32[32,1,2]{2,1,0:T(1,128)}), s32[32,1,2]{2,1,0:T(1,128)S(1)}, u32[]{:S(2)}, u32[]{:S(2)}) async-start(s32[32,1,2]{2,1,0:T(1,128)} %bitcast.2), calls=%async_computation.1 | async-start | bytes 32768 | tf_op jit(solution)/shard_map/all_to_all | solution.py:121
  56.2 28.7 %copy-start.14 = (bf16[192,512]{1,0:T(8,128)(2,1)}, bf16[192,512]{1,0:T(8,128)(2,1)S(1)}, u32[]{:S(2)}) copy-start(bf16[192,512]{1,0:T(8,128)(2,1)S(1)} %collective-permute-done.1) | copy-start | bytes 589828
  56.2 11.4 %collective-permute-start.2 = (bf16[192,512]{1,0:T(8,128)(2,1)S(1)}, bf16[192,512]{1,0:T(8,128)(2,1)S(1)}, u32[]{:S(2)}, u32[]{:S(2)}) collective-permute-start(bf16[192,512]{1,0:T(8,128)(2,1)S(1)} %collective-permute-done.1), channel_id=1, source_target_pairs={{0,7},{1,0},{2,1},{3,2},{4,3},{5,4},{6,5},{7,6},{8,15},{9,8},{10,9... | collective-permute-start | bytes 589832 | tf_op jit(solution)/shard_map/ppermute | solution.py:61
  59.2 25.7 %copy-start.12 = (bf16[192,512]{1,0:T(8,128)(2,1)}, bf16[192,512]{1,0:T(8,128)(2,1)S(1)}, u32[]{:S(2)}) copy-start(bf16[192,512]{1,0:T(8,128)(2,1)S(1)} %collective-permute-done.5) | copy-start | bytes 589828
  59.2 12.2 %collective-permute-start.6 = (bf16[192,512]{1,0:T(8,128)(2,1)S(1)}, bf16[192,512]{1,0:T(8,128)(2,1)S(1)}, u32[]{:S(2)}, u32[]{:S(2)}) collective-permute-start(bf16[192,512]{1,0:T(8,128)(2,1)S(1)} %collective-permute-done.5), channel_id=1, source_target_pairs={{0,1},{1,2},{2,3},{3,4},{4,5},{5,6},{6,7},{7,0},{8,9},{9,10},{10,1... | collective-permute-start | bytes 589832 | tf_op jit(solution)/shard_map/ppermute | solution.py:58
  67.6 17.3 %copy-start.15 = (bf16[192,512]{1,0:T(8,128)(2,1)}, bf16[192,512]{1,0:T(8,128)(2,1)S(1)}, u32[]{:S(2)}) copy-start(bf16[192,512]{1,0:T(8,128)(2,1)S(1)} %collective-permute-done.2) | copy-start | bytes 589828
  84.9 33.1 %all-to-all-start.1 = ((bf16[32,2,16,896]{3,2,1,0:T(8,128)(2,1)}), bf16[32,2,16,896]{3,2,1,0:T(8,128)(2,1)S(1)}, u32[]{:S(2)}, u32[]{:S(2)}) async-start(bf16[32,2,16,896]{3,2,1,0:T(8,128)(2,1)} %bitcast.4), calls=%async_computation.2 | async-start | bytes 3670016 | tf_op jit(solution)/shard_map/all_to_all | solution.py:122
  92.5 132.5 %all-gather.2.cloned.1.call-start = ((), (), s32[]{:S(2)}) async-start(), calls=%async_computation.4 | async-start | bytes 4792320 | tf_op jit(solution)/shard_map/all_gather | solution.py:143
  118.7 36.4 %copy-start.13 = (bf16[192,512]{1,0:T(8,128)(2,1)S(1)}, bf16[192,512]{1,0:T(8,128)(2,1)}, u32[]{:S(2)}) copy-start(bf16[192,512]{1,0:T(8,128)(2,1)} %copy-done.12) | copy-start | bytes 589828
  118.7 59.9 %copy-start.10 = (bf16[192,512]{1,0:T(8,128)(2,1)S(1)}, bf16[192,512]{1,0:T(8,128)(2,1)}, u32[]{:S(2)}) copy-start(bf16[192,512]{1,0:T(8,128)(2,1)} %copy-done.9) | copy-start | bytes 589828
  118.8 60.1 %copy-start.8 = (bf16[192,512]{1,0:T(8,128)(2,1)S(1)}, bf16[192,512]{1,0:T(8,128)(2,1)}, u32[]{:S(2)}) copy-start(bf16[192,512]{1,0:T(8,128)(2,1)} %copy-done.7) | copy-start | bytes 589828
  118.8 33.5 %collective-permute-start.7 = (bf16[24,16,896]{2,1,0:T(8,128)(2,1)S(1)}, bf16[24,16,896]{2,1,0:T(8,128)(2,1)S(1)}, u32[]{:S(2)}, u32[]{:S(2)}) collective-permute-start(bf16[24,16,896]{2,1,0:T(8,128)(2,1)S(1)} %gather_fusion.1), channel_id=1, source_target_pairs={{0,1},{1,2},{2,3},{3,4},{4,5},{5,6},{6,7},{7,0},{8,9},{9,10},{10,1... | collective-permute-start | bytes 2064392 | tf_op jit(solution)/shard_map/ppermute | solution.py:132
  119.3 35.9 %copy-start.3 = (bf16[4096,512]{1,0:T(8,128)(2,1)S(1)}, bf16[4096,512]{1,0:T(8,128)(2,1)}, u32[]{:S(2)}) copy-start(bf16[4096,512]{1,0:T(8,128)(2,1)} %param.13) | copy-start | bytes 12582916
  119.3 59.9 %copy-start.5 = (bf16[192,512]{1,0:T(8,128)(2,1)S(1)}, bf16[192,512]{1,0:T(8,128)(2,1)}, u32[]{:S(2)}) copy-start(bf16[192,512]{1,0:T(8,128)(2,1)} %copy-done.4) | copy-start | bytes 589828
  122.3 33.2 %collective-permute-start.8 = (bf16[24,16,896]{2,1,0:T(8,128)(2,1)S(1)}, bf16[24,16,896]{2,1,0:T(8,128)(2,1)S(1)}, u32[]{:S(2)}, u32[]{:S(2)}) collective-permute-start(bf16[24,16,896]{2,1,0:T(8,128)(2,1)S(1)} %gather_fusion.1), channel_id=1, source_target_pairs={{0,7},{1,0},{2,1},{3,2},{4,3},{5,4},{6,5},{7,6},{8,15},{9,8},{10,9... | collective-permute-start | bytes 2064392 | tf_op jit(solution)/shard_map/ppermute | solution.py:137
  152.3 26.3 %collective-permute-start.9 = (bf16[24,16,896]{2,1,0:T(8,128)(2,1)S(1)}, bf16[24,16,896]{2,1,0:T(8,128)(2,1)S(1)}, u32[]{:S(2)}, u32[]{:S(2)}) collective-permute-start(bf16[24,16,896]{2,1,0:T(8,128)(2,1)S(1)} %collective-permute-done.7), channel_id=1, source_target_pairs={{0,1},{1,2},{2,3},{3,4},{4,5},{5,6},{6,7},{7,0},{8,9},{9,10},{10,1... | collective-permute-start | bytes 2064392 | tf_op jit(solution)/shard_map/ppermute | solution.py:132
  155.5 24.1 %collective-permute-start.10 = (bf16[24,16,896]{2,1,0:T(8,128)(2,1)S(1)}, bf16[24,16,896]{2,1,0:T(8,128)(2,1)S(1)}, u32[]{:S(2)}, u32[]{:S(2)}) collective-permute-start(bf16[24,16,896]{2,1,0:T(8,128)(2,1)S(1)} %collective-permute-done.8), channel_id=1, source_target_pairs={{0,7},{1,0},{2,1},{3,2},{4,3},{5,4},{6,5},{7,6},{8,15},{9,8},{10,9... | collective-permute-start | bytes 2064392 | tf_op jit(solution)/shard_map/ppermute | solution.py:137
  178.6 17.2 %collective-permute-start.11 = (bf16[24,16,896]{2,1,0:T(8,128)(2,1)S(1)}, bf16[24,16,896]{2,1,0:T(8,128)(2,1)S(1)}, u32[]{:S(2)}, u32[]{:S(2)}) collective-permute-start(bf16[24,16,896]{2,1,0:T(8,128)(2,1)S(1)} %collective-permute-done.9), channel_id=1, source_target_pairs={{0,1},{1,2},{2,3},{3,4},{4,5},{5,6},{6,7},{7,0},{8,9},{9,10},{10,1... | collective-permute-start | bytes 2064392 | tf_op jit(solution)/shard_map/ppermute | solution.py:132
  179.5 17.0 %collective-permute-start.12 = (bf16[24,16,896]{2,1,0:T(8,128)(2,1)S(1)}, bf16[24,16,896]{2,1,0:T(8,128)(2,1)S(1)}, u32[]{:S(2)}, u32[]{:S(2)}) collective-permute-start(bf16[24,16,896]{2,1,0:T(8,128)(2,1)S(1)} %collective-permute-done.10), channel_id=1, source_target_pairs={{0,7},{1,0},{2,1},{3,2},{4,3},{5,4},{6,5},{7,6},{8,15},{9,8},{10,9... | collective-permute-start | bytes 2064392 | tf_op jit(solution)/shard_map/ppermute | solution.py:137
  195.9 16.4 %collective-permute-start.13 = (bf16[24,16,896]{2,1,0:T(8,128)(2,1)S(1)}, bf16[24,16,896]{2,1,0:T(8,128)(2,1)S(1)}, u32[]{:S(2)}, u32[]{:S(2)}) collective-permute-start(bf16[24,16,896]{2,1,0:T(8,128)(2,1)S(1)} %collective-permute-done.11), channel_id=1, source_target_pairs={{0,1},{1,2},{2,3},{3,4},{4,5},{5,6},{6,7},{7,0},{8,9},{9,10},{10,1... | collective-permute-start | bytes 2064392 | tf_op jit(solution)/shard_map/ppermute | solution.py:132
  (8 other events, 19.8 us)
Sparse Core Ops, SparseCore 0:
  17.4 64.0 reduce-scatter.1
  95.2 76.5 all-gather.1
